TPU v7x, 128 devices: a whole 4x4x4 slice. The times are simulated.
128 devices in a mesh: seq: 16 (over z, x_hi, core), head: 8 (over y, x_lo).
Axes of the slice: x: 4 (x_hi: 2, x_lo: 2; x = x_hi * 2 + x_lo), y: 4, z: 4, core: 2. Of those that a mesh axis runs over, the one named last changes fastest.
Arguments:
- queries: bfloat16 [16384, 4096], P('seq', 'head'), may hold values from -6 to 6
- key_rows: bfloat16 [16384, 4096], P('seq', 'head'), may hold values from -6 to 6
- value_rows: bfloat16 [16384, 4096], P('seq', 'head'), may hold values from -6 to 6
- out_weight: bfloat16 [4096, 4096], P('head'), may hold values from -0.375 to 0.375
- cotangent: bfloat16 [16384, 4096], P('seq', 'head'), may hold values from -1.5 to 1.5
- pattern: int32 [128, 7], P('seq'), may hold values 0 or 1
Outputs:
- output: bfloat16 [16384, 4096], P('seq', 'head')
- grad_query: bfloat16 [16384, 4096], P('seq', 'head')
- grad_keys: bfloat16 [16384, 4096], P('seq', 'head')
- grad_values: bfloat16 [16384, 4096], P('seq', 'head')
- grad_weight: float32 [4096, 4096], P('seq', 'head')
All inputs are finite; a program needn't handle non-finite values. No bound on the sum of `pattern` on one device may be relied on, other than what follows from the above.
Results may differ from a plain program's by a relative error of at most 0.0076.
Values may be sent and summed in bfloat16 or wider, within the bound.
No kernel may reach another device: no remote copies, remote signals or barrier semaphores. Data moves between devices by JAX's collectives and lax.ppermute only.
A program may use at most 256 MiB of HBM per device.

v0:
```python
import math
import jax
import jax.numpy as jnp
from jax import lax
from jax.sharding import PartitionSpec as P

DH = 128
BLK = 128
LOG_TWO = math.log(2.0)


def swapped(value, axis, bit):
    mask = 2**bit
    pairs = [(source, source ^ mask) for source in range(lax.axis_size(axis))]
    return lax.ppermute(value, axis, pairs)


def pair_mean(tensor):
    shape_in = tensor.shape
    paired = tensor.reshape(shape_in[:-2] + (shape_in[-2] // 2, 2, shape_in[-1]))
    return jnp.sum(paired, axis=-2) * 0.5


def spread_rows(grads, factor):
    shape_in = grads.shape
    wide = jnp.broadcast_to(grads[..., :, None, :], shape_in[:-1] + (factor, shape_in[-1])) * (
        1.0 / factor
    )
    return wide.reshape(shape_in[:-2] + (shape_in[-2] * factor, shape_in[-1]))


def head_ring_gather(value, relative=False):
    count = lax.axis_size("head")
    rings = count // 2
    width = value.shape[-1]
    where_head = lax.axis_index("head")
    ring_pos = where_head // 2
    partner = lax.ppermute(value, "head", [(src, src ^ 1) for src in range(count)])
    low_first = where_head % 2 == 0
    if relative:
        pair_block = jnp.concatenate([value, partner], axis=-1)
    else:
        pair_block = jnp.concatenate(
            [jnp.where(low_first, value, partner), jnp.where(low_first, partner, value)], axis=-1
        )
    upward = [(src, (src // 2 + 1) % rings * 2 + src % 2) for src in range(count)]
    downward = [(src, (src // 2 - 1) % rings * 2 + src % 2) for src in range(count)]
    from_below = lax.ppermute(pair_block, "head", upward)
    from_above = lax.ppermute(pair_block, "head", downward)
    blocks = [pair_block, from_above]
    if rings == 4:
        far = jnp.concatenate(
            [
                lax.ppermute(from_below[..., :width], "head", upward),
                lax.ppermute(from_above[..., width:], "head", downward),
            ],
            axis=-1,
        )
        blocks = [pair_block, from_above, far, from_below]
    if relative:
        return blocks
    stacked = jnp.stack(blocks)
    order = (jnp.arange(rings) - ring_pos) % rings
    placed = stacked[order]
    return jnp.moveaxis(placed, 0, -2).reshape(value.shape[:-1] + (rings * 2 * width,))


def weight_columns(out_weight):
    count = lax.axis_size("head")
    seq_count = lax.axis_size("seq")
    where_head = lax.axis_index("head")
    core = lax.axis_index("seq") % 2
    rows, cols = out_weight.shape
    width = cols // count
    own = lax.dynamic_slice_in_dim(out_weight, where_head * width, width, axis=1)
    fetched = []
    for step in range(count // 2):
        shift_low, shift_high = (2 * step + 1, 2 * step + 2)
        pairs = []
        for seq_idx in range(seq_count):
            shift = shift_low if seq_idx % 2 == 0 else shift_high
            if shift % count == 0:
                continue
            for src in range(count):
                pairs.append((seq_idx * count + src, seq_idx * count + (src + shift) % count))
        shift = jnp.where(core == 0, shift_low, shift_high)
        outgoing = lax.dynamic_slice_in_dim(
            out_weight, (where_head + shift) % count * width, width, axis=1
        )
        fetched.append(lax.ppermute(outgoing, ("seq", "head"), pairs))
    mine = jnp.stack(fetched)
    theirs = lax.ppermute(mine, "seq", [(src, src ^ 1) for src in range(seq_count)])
    odd = jnp.where(core == 0, mine, theirs)
    even = jnp.where(core == 0, theirs, mine)
    by_shift = [own]
    for shift in range(1, count):
        by_shift.append(odd[(shift - 1) // 2] if shift % 2 else even[shift // 2 - 1])
    low_first = where_head % 2 == 0
    ring_blocks = []
    for dist in range(count // 2):
        ring_blocks.append(
            jnp.concatenate(
                [
                    by_shift[-2 * dist % count],
                    jnp.where(
                        low_first,
                        by_shift[(-1 - 2 * dist) % count],
                        by_shift[(1 - 2 * dist) % count],
                    ),
                ],
                axis=0,
            )
        )
    return ring_blocks


def body(queries, key_rows, value_rows, out_weight, cotangent, pattern):
    row_count, features = queries.shape
    blocks = row_count // BLK
    local_levels = blocks.bit_length() - 1
    seq_count = lax.axis_size("seq")
    cross_levels = seq_count.bit_length() - 1
    level_count = local_levels + cross_levels
    head_count = features // DH
    keys_all = (1 + level_count) * BLK
    score_scale = DH ** (-0.5)
    where_seq = lax.axis_index("seq")
    stacked = jnp.stack([key_rows, value_rows])
    coarse_base = (
        stacked.reshape(2, BLK, row_count // BLK, features).astype(jnp.float32).mean(axis=2)
    )
    siblings = []
    current = coarse_base
    for level_idx in range(cross_levels):
        received = swapped(current, "seq", level_idx)
        siblings.append(received)
        if level_idx + 1 < cross_levels:
            upper_half = jnp.right_shift(where_seq, level_idx) & 1 == 1
            joined = jnp.where(
                upper_half,
                jnp.concatenate([received, current], axis=1),
                jnp.concatenate([current, received], axis=1),
            )
            current = pair_mean(joined)
    segments = [stacked.reshape(2, blocks, BLK, features)]
    for level_idx in range(local_levels):
        factor = 2**level_idx
        group_count = blocks >> level_idx
        if level_idx == 0:
            pooled = stacked
        else:
            pooled = (
                stacked.reshape(2, row_count // factor, factor, features)
                .astype(jnp.float32)
                .mean(axis=2)
                .astype(jnp.bfloat16)
            )
        paired = pooled.reshape(2, group_count // 2, 2, BLK, features)
        sibling = jnp.concatenate([paired[:, :, 1:], paired[:, :, :1]], axis=2).reshape(
            2, group_count, BLK, features
        )
        segments.append(
            jnp.broadcast_to(sibling[:, :, None], (2, group_count, factor, BLK, features)).reshape(
                2, blocks, BLK, features
            )
        )
    key_set = jnp.concatenate(segments, axis=2)
    far_set = jnp.concatenate(
        [siblings[level_idx].astype(jnp.bfloat16) for level_idx in range(cross_levels)], axis=1
    )
    near_keys = (1 + local_levels) * BLK
    far_keys = cross_levels * BLK
    key_bias = jnp.concatenate(
        [jnp.zeros((BLK,), jnp.float32)]
        + [jnp.full((BLK,), level_idx * LOG_TWO, jnp.float32) for level_idx in range(level_count)]
    )
    level_flags = pattern == 1
    kept_mask = jnp.concatenate(
        [
            jnp.ones((blocks, BLK), bool),
            jnp.broadcast_to(level_flags[:, :, None], (blocks, level_count, BLK)).reshape(
                blocks, level_count * BLK
            ),
        ],
        axis=1,
    )
    query_heads = queries.reshape(blocks, BLK, head_count, DH)
    key_heads = key_set[0].reshape(blocks, near_keys, head_count, DH)
    value_heads = key_set[1].reshape(blocks, near_keys, head_count, DH)
    far_key_heads = far_set[0].reshape(far_keys, head_count, DH)
    far_value_heads = far_set[1].reshape(far_keys, head_count, DH)
    scores = (
        jnp.concatenate(
            [
                jnp.einsum(
                    "bqhd,bkhd->bhqk", query_heads, key_heads, preferred_element_type=jnp.float32
                ),
                jnp.einsum(
                    "bqhd,khd->bhqk", query_heads, far_key_heads, preferred_element_type=jnp.float32
                ),
            ],
            axis=-1,
        )
        * score_scale
        + key_bias
    )
    scores = jnp.where(kept_mask[:, None, None, :], scores, -jnp.inf)
    row_max = jnp.max(scores, axis=-1, keepdims=True)
    weights_raw = jnp.exp(scores - row_max)
    attn_prob = weights_raw / jnp.sum(weights_raw, axis=-1, keepdims=True)
    prob_low = attn_prob.astype(jnp.bfloat16)
    near_prob, far_prob = (prob_low[..., :near_keys], prob_low[..., near_keys:])
    mixed = jnp.einsum(
        "bhqk,bkhd->bqhd", near_prob, value_heads, preferred_element_type=jnp.float32
    ) + jnp.einsum("bhqk,khd->bqhd", far_prob, far_value_heads, preferred_element_type=jnp.float32)
    attended = mixed.astype(jnp.bfloat16).reshape(row_count, features)
    attended, weight_cols = lax.optimization_barrier((attended, weight_columns(out_weight)))
    half_rows = row_count // 2
    grads_full = jnp.concatenate(
        [
            lax.all_gather(cotangent[:half_rows], "head", axis=1, tiled=True),
            head_ring_gather(cotangent[half_rows:]),
        ],
        axis=0,
    )
    grad_attn = lax.dot_general(
        grads_full, out_weight, (((1,), (1,)), ((), ())), preferred_element_type=jnp.float32
    ).astype(jnp.bfloat16)
    late_attended, grad_attn = lax.optimization_barrier((attended, grad_attn))
    attended_blocks = head_ring_gather(late_attended, relative=True)
    grad_weight = lax.psum_scatter(
        lax.dot_general(
            grads_full, attended, (((0,), (0,)), ((), ())), preferred_element_type=jnp.float32
        ),
        "seq",
        scatter_dimension=0,
        tiled=True,
    )
    grad_heads = grad_attn.reshape(blocks, BLK, head_count, DH)
    grad_prob = jnp.concatenate(
        [
            jnp.einsum(
                "bqhd,bkhd->bhqk", grad_heads, value_heads, preferred_element_type=jnp.float32
            ),
            jnp.einsum(
                "bqhd,khd->bhqk", grad_heads, far_value_heads, preferred_element_type=jnp.float32
            ),
        ],
        axis=-1,
    )
    row_delta = jnp.sum(attn_prob * grad_prob, axis=-1, keepdims=True)
    grad_score = (attn_prob * (grad_prob - row_delta)).astype(jnp.bfloat16)
    near_score, far_score = (grad_score[..., :near_keys], grad_score[..., near_keys:])
    grad_query = (
        (
            (
                jnp.einsum(
                    "bhqk,bkhd->bqhd", near_score, key_heads, preferred_element_type=jnp.float32
                )
                + jnp.einsum(
                    "bhqk,khd->bqhd", far_score, far_key_heads, preferred_element_type=jnp.float32
                )
            )
            * score_scale
        )
        .astype(jnp.bfloat16)
        .reshape(row_count, features)
    )
    grad_keyset = (
        jnp.einsum("bhqk,bqhd->bkhd", near_score, query_heads, preferred_element_type=jnp.float32)
        * score_scale
    )
    grad_valset = jnp.einsum(
        "bhqk,bqhd->bkhd", near_prob, grad_heads, preferred_element_type=jnp.float32
    )
    grad_sets = jnp.stack([grad_keyset, grad_valset]).reshape(2, blocks, near_keys, features)
    far_grad_keys = (
        jnp.einsum("bhqk,bqhd->khd", far_score, query_heads, preferred_element_type=jnp.float32)
        * score_scale
    )
    far_grad_values = jnp.einsum(
        "bhqk,bqhd->khd", far_prob, grad_heads, preferred_element_type=jnp.float32
    )
    far_grads = jnp.stack([far_grad_keys, far_grad_values]).reshape(2, far_keys, features)
    token_grad = grad_sets[:, :, :BLK].reshape(2, row_count, features)
    level_grads = []
    for level_idx in range(local_levels):
        factor = 2**level_idx
        group_count = blocks >> level_idx
        lower = (level_idx + 1) * BLK
        segment = (
            grad_sets[:, :, lower : lower + BLK]
            .reshape(2, group_count, factor, BLK, features)
            .sum(axis=2)
        )
        paired = segment.reshape(2, group_count // 2, 2, BLK, features)
        restored = jnp.concatenate([paired[:, :, 1:], paired[:, :, :1]], axis=2).reshape(
            2, group_count * BLK, features
        )
        level_grads.append(restored)
    sibling_grads = []
    for level_idx in range(cross_levels):
        sibling_grads.append(far_grads[:, level_idx * BLK : (level_idx + 1) * BLK])
    carried = jnp.zeros((2, BLK, features), jnp.float32)
    for level_idx in reversed(range(cross_levels)):
        outgoing = sibling_grads[level_idx]
        if level_idx + 1 < cross_levels:
            halves = spread_rows(carried, 2)
            lower_part = halves[:, :BLK]
            upper_part = halves[:, BLK:]
            upper_half = jnp.right_shift(where_seq, level_idx) & 1 == 1
            own_part = jnp.where(upper_half, upper_part, lower_part)
            outgoing = outgoing + jnp.where(upper_half, lower_part, upper_part)
        else:
            own_part = jnp.zeros_like(outgoing)
        carried = own_part + swapped(outgoing, "seq", level_idx)
    attended_blocks, carried = lax.optimization_barrier((attended_blocks, carried))
    output_sum = jnp.dot(attended_blocks[0], weight_cols[0], preferred_element_type=jnp.float32)
    for dist in range(1, len(attended_blocks)):
        output_sum = output_sum + jnp.dot(
            attended_blocks[dist], weight_cols[dist], preferred_element_type=jnp.float32
        )
    output = output_sum.astype(jnp.bfloat16)
    if local_levels:
        pooled_grad = level_grads[-1]
        for level_idx in reversed(range(local_levels - 1)):
            pooled_grad = level_grads[level_idx] + spread_rows(pooled_grad, 2)
        token_grad = token_grad + pooled_grad
    token_grad = token_grad + spread_rows(carried, 2**local_levels)
    grad_keys = token_grad[0].astype(jnp.bfloat16)
    grad_values = token_grad[1].astype(jnp.bfloat16)
    return (output, grad_query, grad_keys, grad_values, grad_weight)


def solution(mesh):
    placed = (
        P("seq", "head"),
        P("seq", "head"),
        P("seq", "head"),
        P("head", None),
        P("seq", "head"),
        P("seq", None),
    )
    return jax.shard_map(
        body,
        mesh=mesh,
        in_specs=placed,
        out_specs=(
            P("seq", "head"),
            P("seq", "head"),
            P("seq", "head"),
            P("seq", "head"),
            P("seq", "head"),
        ),
        check_vma=False,
    )
```

profile of v0, /device:TPU:0, one launch (start us, length us, event | category | flops | bytes accessed | tf_op | source)
XLA Modules:
  0.0 408.6 jit_solution(15762008881767522509)
XLA Ops:
  30.9 5.8 %convert_reduce_fusion.2 = f32[2,512,512]{2,1,0:T(8,128)S(1)} fusion(bf16[1,512,2,512]{3,2,1,0:T(2,128)(2,1)S(1)} %copy-done.28, bf16[1,512,2,512]{3,2,1,0:T(2,128)(2,1)S(1)} %copy-done.27), kind=kLoop, calls=%fused_computation.42 | loop fusion | flops 2621440 | bytes 4194304 | tf_op jit(solution)/shard_map/reduce_sum | solution.py:155
  45.0 6.6 %copy.194 = bf16[1,8,512,512]{2,3,1,0:T(8,128)(2,1)} copy(bf16[1,8,512,512]{3,2,1,0:T(8,128)(2,1)} %get-tuple-element.54) | data formatting | bytes 8388608 | tf_op jit(solution)/shard_map/slice | solution.py:188
  58.0 4.6 %convolution_bitcast_fusion.2 = f32[8,4,128,512]{2,3,1,0:T(8,128)} fusion(bf16[8,512,4,128]{1,3,2,0:T(8,128)(2,1)S(1)} %bitcast.165, bf16[8,128,4,128]{1,3,2,0:T(8,128)(2,1)S(1)} %copy.218), kind=kOutput, calls=%fused_computation.57 | convolution fusion | flops 536870912 | bytes 13631488 | tf_op jit(solution)/shard_map/bqhd,bkhd->bhqk/dot_general | solution.py:195
  62.7 8.1 %collective-permute-done.1 = f32[2,128,512]{2,1,0:T(8,128)S(1)} collective-permute-done((f32[2,128,512]{2,1,0:T(8,128)S(1)}, f32[2,128,512]{2,1,0:T(8,128)S(1)}, u32[]{:S(2)}, u32[]{:S(2)}) %collective-permute-start.1) | collective-permute-done | bytes 524320 | tf_op jit(solution)/shard_map/ppermute | solution.py:15
  80.5 6.5 %copy.192 = bf16[1,8,512,512]{2,3,1,0:T(8,128)(2,1)} copy(bf16[1,8,512,512]{3,2,1,0:T(8,128)(2,1)} %get-tuple-element.53) | data formatting | bytes 8388608 | tf_op jit(solution)/shard_map/slice | solution.py:189
  89.6 5.5 %collective-permute-start.7 = (bf16[512,512]{1,0:T(8,128)(2,1)}, bf16[512,512]{1,0:T(8,128)(2,1)}, u32[]{:S(2)}, u32[]{:S(2)}) collective-permute-start(bf16[512,512]{1,0:T(8,128)(2,1)} %get-tuple-element.63), channel_id=1, source_target_pairs={{0,7},{1,0},{2,1},{3,2},{4,3},{5,4},{6,5},{7,6},{16,23},{17,16},{1... | collective-permute-start | bytes 1572872 | tf_op jit(solution)/shard_map/ppermute | solution.py:90
  105.8 17.4 %collective-permute-start.8 = (bf16[4,512,512]{2,1,0:T(8,128)(2,1)}, bf16[4,512,512]{2,1,0:T(8,128)(2,1)}, u32[]{:S(2)}, u32[]{:S(2)}) collective-permute-start(bf16[4,512,512]{2,1,0:T(8,128)(2,1)} %pad_maximum_fusion.10), channel_id=1, source_target_pairs={{0,8},{8,0},{16,24},{24,16},{32,40},{40,32},{48,56},{56,48},{64,72... | collective-permute-start | bytes 6291464 | tf_op jit(solution)/shard_map/ppermute | solution.py:92
  134.2 7.9 %fusion.81 = (f32[8,4,128]{2,1,0:T(4,128)S(1)}, f32[8,4,128,1024]{2,3,1,0:T(8,128)S(1)}) fusion(f32[8,4,128,512]{2,3,1,0:T(8,128)S(1)} %convolution_bitcast_fusion.1, f32[8,4,128,512]{2,3,1,0:T(8,128)} %convolution_bitcast_fusion.2, f32[1024]{0:T(1024)S(1)} %copy-done.46, pred[8,1024]{1,0:T(8,128)(4,1)S(1)} %concatenate.89), kind=kOutput, calls=%fused_computation.168 | output fusion | flops 25166848 | bytes 33583104 | tf_op jit(solution)/shard_map/sub | solution.py:209
  146.2 4.2 %copy-done.12 = f32[8,4,128,1024]{2,3,1,0:T(8,128)} copy-done((f32[8,4,128,1024]{2,3,1,0:T(8,128)}, f32[8,4,128,1024]{2,3,1,0:T(8,128)S(1)}, u32[]{:S(2)}) %copy-start.12) | copy-done | bytes 16777240
  163.4 5.0 %gather_fusion = bf16[4,512,1024]{2,1,0:T(8,128)(2,1)} fusion(bf16[4,512,1024]{2,1,0:T(8,128)(2,1)} %pad_maximum_fusion.7, s32[1024]{0:T(1024)S(1)} %pad_clamp_fusion), kind=kCustom, calls=%fused_computation | custom fusion | bytes 8388624 | tf_op jit(solution)/shard_map/gather | solution.py:64
  168.4 6.3 %copy.211 = bf16[512,4,1024]{0,2,1:T(8,128)(2,1)} copy(bf16[512,4,1024]{2,0,1:T(8,128)(2,1)} %bitcast.179) | data formatting | bytes 8388608 | tf_op jit(solution)/shard_map/transpose | solution.py:65
  181.9 8.6 %all-gather.2.cloned.1.call-done = bf16[512,4096]{0,1:T(8,128)(2,1)} async-done(((bf16[512,512]{0,1:T(8,128)(2,1)}), bf16[512,4096]{0,1:T(8,128)(2,1)}) %all-gather.2.cloned.1.call-update) | async-done | bytes 4194320 | tf_op jit(solution)/shard_map/all_gather | solution.py:221
  190.5 9.2 %fusion.45 = bf16[1024,512]{1,0:T(8,128)(2,1)S(1)} fusion(bf16[512,4096]{1,0:T(8,128)(2,1)} %param.9, bf16[512,4096]{0,1:T(8,128)(2,1)} %bitcast.194, bf16[512,4096]{0,1:T(8,128)(2,1)} %all-gather.2.cloned.1.call-done), kind=kOutput, calls=%fused_computation.82 | convolution fusion | flops 4312268800 | bytes 13631488 | tf_op jit(solution)/shard_map/dot_general | solution.py:226
  200.7 5.1 %fusion.20 = f32[4,128,512,1]{2,1,3,0:T(8,128)} fusion(bf16[8,128,4,128]{3,2,1,0:T(4,128)(2,1)S(1)} %reshape.240, bf16[8,4,128,1024]{2,3,1,0:T(8,128)(2,1)} %fusion.70), kind=kOutput, calls=%fused_computation.37 | convolution fusion | flops 536870912 | bytes 6291456 | tf_op jit(solution)/shard_map/bhqk,bqhd->khd/dot_general | solution.py:281
  205.8 4.6 %fusion.82 = f32[8,4,128,512]{2,3,1,0:T(8,128)} fusion(bf16[8,128,4,128]{1,3,2,0:T(8,128)(2,1)S(1)} %copy.237, bf16[8,512,4,128]{1,3,2,0:T(8,128)(2,1)S(1)} %bitcast.176), kind=kOutput, calls=%fused_computation.169 | convolution fusion | flops 536870912 | bytes 13631488 | tf_op jit(solution)/shard_map/bqhd,bkhd->bhqk/dot_general | solution.py:242
  210.5 5.5 %convolution_bitcast_fusion = f32[8,4,128,512]{2,3,1,0:T(8,128)} fusion(bf16[512,4,128,1]{0,2,1,3:T(8,128)(2,1)S(1)} %bitcast.188, bf16[8,128,4,128]{1,3,2,0:T(8,128)(2,1)S(1)} %copy.237), kind=kOutput, calls=%fused_computation.55 | convolution fusion | flops 536870912 | bytes 9961472 | tf_op jit(solution)/shard_map/bqhd,khd->bhqk/dot_general | solution.py:245
  216.8 8.3 %fusion.13 = f32[4096,512]{1,0:T(8,128)} fusion(bf16[1024,512]{0,1:T(8,128)(2,1)} %bitcast.164, bf16[512,4096]{0,1:T(8,128)(2,1)S(1)} %bitcast.195, bf16[512,4096]{0,1:T(8,128)(2,1)S(1)} %copy-done.45), kind=kOutput, calls=%fused_computation.25 | convolution fusion | flops 4311744512 | bytes 17825792 | tf_op jit(solution)/shard_map/dot_general | solution.py:232
  227.0 29.6 %multiply_convert_fusion = bf16[8,4,128,1024]{2,3,1,0:T(8,128)(2,1)} fusion(f32[8,4,128,512]{2,3,1,0:T(8,128)} %convolution_bitcast_fusion, f32[8,4,128,512]{2,3,1,0:T(8,128)} %fusion.82, f32[8,4,128,1024]{2,3,1,0:T(8,128)} %copy-done.12, f32[8,4,128]{2,1,0:T(4,128)S(1)} %get-tuple-element.94), kind=kOutput, calls=%fused_computation.13 | output fusion | flops 33559552 | bytes 41959424 | tf_op jit(solution)/shard_map/sub | solution.py:252
  256.6 4.6 %fusion.49 = f32[4,512,128]{1,2,0:T(8,128)} fusion(bf16[8,128,4,128]{1,3,2,0:T(8,128)(2,1)S(1)} %copy-done.9, bf16[8,4,128,1024]{2,3,1,0:T(8,128)(2,1)} %multiply_convert_fusion), kind=kOutput, calls=%fused_computation.84 | convolution fusion | flops 537133056 | bytes 6291456 | tf_op jit(solution)/shard_map/bhqk,bqhd->khd/dot_general | solution.py:278
  273.7 7.0 %fusion.16 = (f32[2,8,128,512]{2,3,1,0:T(8,128)}, f32[2,8,128,512]{2,3,1,0:T(8,128)}, f32[2,8,128,512]{2,3,1,0:T(8,128)}, f32[2,8,128,512]{2,3,1,0:T(8,128)}) fusion(f32[1,8,512,512]{2,3,1,0:T(8,128)S(1)} %bitcast.178, f32[1,8,512,512]{2,3,1,0:T(8,128)S(1)} %bitcast.177), kind=kLoop, calls=%fused_computation.28 | loop fusion | flops 4194304 | bytes 33554432 | tf_op jit(solution)/shard_map/stack | solution.py:276
  284.4 4.2 %fusion.39 = bf16[8,128,4,128]{1,3,2,0:T(8,128)(2,1)} fusion(f32[8,4,128,128]{3,2,1,0:T(8,128)S(1)} %fusion.24, bf16[512,4,128,1]{0,2,1,3:T(8,128)(2,1)S(1)} %bitcast.190, bf16[8,4,128,1024]{2,3,1,0:T(8,128)(2,1)} %multiply_convert_fusion), kind=kOutput, calls=%fused_computation.75 | convolution fusion | flops 538443776 | bytes 7864320 | tf_op jit(solution)/shard_map/bhqk,khd->bqhd/dot_general | solution.py:260
  305.9 4.4 %collective-permute-done.20 = f32[2,128,512]{2,1,0:T(8,128)S(1)} collective-permute-done((f32[2,128,512]{2,1,0:T(8,128)S(1)}, f32[2,128,512]{2,1,0:T(8,128)S(1)}, u32[]{:S(2)}, u32[]{:S(2)}) %collective-permute-start.20) | collective-permute-done | bytes 524320 | tf_op jit(solution)/shard_map/ppermute | solution.py:15
  321.4 5.4 %copy.239 = f32[2,8,128,512]{3,2,1,0:T(8,128)} copy(f32[2,8,128,512]{2,3,1,0:T(8,128)} %get-tuple-element.49) | data formatting | bytes 8388608 | tf_op jit(solution)/shard_map/slice | solution.py:285
  368.8 6.3 %reshape.254 = f32[2,1024,512]{2,1,0:T(8,128)} reshape(f32[2,512,2,512]{3,2,1,0:T(2,128)} %broadcast_in_dim.45) | data formatting | bytes 8388608 | tf_op jit(solution)/shard_map/reshape | solution.py:29
  (260 shorter events, 212.5 us)
Async XLA Ops:
  7.2 183.4 %all-gather.2.cloned.1.call-start = ((), (), s32[]{:S(2)}) async-start(), calls=%async_computation.1 | async-start | bytes 4718592 | tf_op jit(solution)/shard_map/all_gather | solution.py:221
  9.1 65.8 %collective-permute-start.9 = (bf16[512,512]{1,0:T(8,128)(2,1)}, bf16[512,512]{1,0:T(8,128)(2,1)}, u32[]{:S(2)}, u32[]{:S(2)}) collective-permute-start(bf16[512,512]{1,0:T(8,128)(2,1)} %slice.169), channel_id=1, source_target_pairs={{0,1},{1,0},{2,3},{3,2},{4,5},{5,4},{6,7},{7,6},{8,9},{9,8},{10,11... | collective-permute-start | bytes 1572872 | tf_op jit(solution)/shard_map/ppermute | solution.py:38
  14.6 37.1 %collective-permute-start = (f32[2,128,512]{2,1,0:T(8,128)}, f32[2,128,512]{2,1,0:T(8,128)}, u32[]{:S(2)}, u32[]{:S(2)}) collective-permute-start(f32[2,128,512]{2,1,0:T(8,128)} %broadcast_multiply_fusion.3), channel_id=1, source_target_pairs={{0,8},{8,0},{16,24},{24,16},{32,40},{40,32},{48,56},{56,48},{64,72... | collective-permute-start | bytes 1572872 | tf_op jit(solution)/shard_map/ppermute | solution.py:15
  17.9 71.7 %collective-permute-start.6 = (bf16[512,512]{1,0:T(8,128)(2,1)}, bf16[512,512]{1,0:T(8,128)(2,1)}, u32[]{:S(2)}, u32[]{:S(2)}) collective-permute-start(bf16[512,512]{1,0:T(8,128)(2,1)} %get-tuple-element.60), channel_id=1, source_target_pairs={{0,5},{1,6},{2,7},{3,0},{4,1},{5,2},{6,3},{7,4},{8,14},{9,15},{10,... | collective-permute-start | bytes 1572872 | tf_op jit(solution)/shard_map/ppermute | solution.py:90
  21.1 75.3 %collective-permute-start.5 = (bf16[512,512]{1,0:T(8,128)(2,1)}, bf16[512,512]{1,0:T(8,128)(2,1)}, u32[]{:S(2)}, u32[]{:S(2)}) collective-permute-start(bf16[512,512]{1,0:T(8,128)(2,1)} %get-tuple-element.61), channel_id=1, source_target_pairs={{0,3},{1,4},{2,5},{3,6},{4,7},{5,0},{6,1},{7,2},{8,12},{9,13},{10,... | collective-permute-start | bytes 1572872 | tf_op jit(solution)/shard_map/ppermute | solution.py:90
  54.9 15.8 %collective-permute-start.1 = (f32[2,128,512]{2,1,0:T(8,128)S(1)}, f32[2,128,512]{2,1,0:T(8,128)S(1)}, u32[]{:S(2)}, u32[]{:S(2)}) collective-permute-start(f32[2,128,512]{2,1,0:T(8,128)S(1)} %copy_multiply_fusion.2), channel_id=1, source_target_pairs={{0,16},{8,24},{16,0},{24,8},{32,48},{40,56},{48,32},{56,40},{64,80... | collective-permute-start | bytes 1572872 | tf_op jit(solution)/shard_map/ppermute | solution.py:15
  73.0 14.0 %collective-permute-start.2 = (f32[2,128,512]{2,1,0:T(8,128)}, f32[2,128,512]{2,1,0:T(8,128)}, u32[]{:S(2)}, u32[]{:S(2)}) collective-permute-start(f32[2,128,512]{2,1,0:T(8,128)} %copy_multiply_fusion.1), channel_id=1, source_target_pairs={{0,32},{8,40},{16,48},{24,56},{32,0},{40,8},{48,16},{56,24},{64,96... | collective-permute-start | bytes 1572872 | tf_op jit(solution)/shard_map/ppermute | solution.py:15
  78.4 45.9 %collective-permute-start.10 = (bf16[512,1024]{1,0:T(8,128)(2,1)}, bf16[512,1024]{1,0:T(8,128)(2,1)S(1)}, u32[]{:S(2)}, u32[]{:S(2)}) collective-permute-start(bf16[512,1024]{1,0:T(8,128)(2,1)} %get-tuple-element.87), channel_id=1, source_target_pairs={{0,6},{1,7},{2,0},{3,1},{4,2},{5,3},{6,4},{7,5},{8,14},{9,15},{10,... | collective-permute-start | bytes 3145736 | tf_op jit(solution)/shard_map/ppermute | solution.py:49
  79.5 47.8 %collective-permute-start.11 = (bf16[512,1024]{1,0:T(8,128)(2,1)}, bf16[512,1024]{1,0:T(8,128)(2,1)S(1)}, u32[]{:S(2)}, u32[]{:S(2)}) collective-permute-start(bf16[512,1024]{1,0:T(8,128)(2,1)} %get-tuple-element.87), channel_id=1, source_target_pairs={{0,2},{1,3},{2,4},{3,5},{4,6},{5,7},{6,0},{7,1},{8,10},{9,11},{10,... | collective-permute-start | bytes 3145736 | tf_op jit(solution)/shard_map/ppermute | solution.py:48
  87.0 15.2 %collective-permute-start.4 = (bf16[512,512]{1,0:T(8,128)(2,1)}, bf16[512,512]{1,0:T(8,128)(2,1)}, u32[]{:S(2)}, u32[]{:S(2)}) collective-permute-start(bf16[512,512]{1,0:T(8,128)(2,1)} %get-tuple-element.62), channel_id=1, source_target_pairs={{0,1},{1,2},{2,3},{3,4},{4,5},{5,6},{6,7},{7,0},{8,10},{9,11},{10,... | collective-permute-start | bytes 1572872 | tf_op jit(solution)/shard_map/ppermute | solution.py:90
  96.4 33.1 %collective-permute-start.3 = (bf16[2,128,512]{2,1,0:T(8,128)(2,1)S(1)}, bf16[2,128,512]{2,1,0:T(8,128)(2,1)}, u32[]{:S(2)}, u32[]{:S(2)}) collective-permute-start(bf16[2,128,512]{2,1,0:T(8,128)(2,1)S(1)} %copy_multiply_fusion), channel_id=1, source_target_pairs={{0,64},{8,72},{16,80},{24,88},{32,96},{40,104},{48,112},{56,120},{... | collective-permute-start | bytes 786440 | tf_op jit(solution)/shard_map/ppermute | solution.py:15
  102.2 299.3 %reduce-scatter.2.cloned.1.call-start = ((), (), s32[]{:S(2)}) async-start(), calls=%async_computation.2 | async-start | bytes 8912896 | tf_op jit(solution)/shard_map/reduce_scatter | solution.py:231
  105.8 68.8 %collective-permute-start.8 = (bf16[4,512,512]{2,1,0:T(8,128)(2,1)}, bf16[4,512,512]{2,1,0:T(8,128)(2,1)}, u32[]{:S(2)}, u32[]{:S(2)}) collective-permute-start(bf16[4,512,512]{2,1,0:T(8,128)(2,1)} %pad_maximum_fusion.10), channel_id=1, source_target_pairs={{0,8},{8,0},{16,24},{24,16},{32,40},{40,32},{48,56},{56,48},{64,72... | collective-permute-start | bytes 6291464 | tf_op jit(solution)/shard_map/ppermute | solution.py:92
  125.3 34.3 %collective-permute-start.13 = (bf16[512,512]{1,0:T(8,128)(2,1)}, bf16[512,512]{1,0:T(8,128)(2,1)}, u32[]{:S(2)}, u32[]{:S(2)}) collective-permute-start(bf16[512,512]{1,0:T(8,128)(2,1)} %slice.220), channel_id=1, source_target_pairs={{0,6},{1,7},{2,0},{3,1},{4,2},{5,3},{6,4},{7,5},{8,14},{9,15},{10,... | collective-permute-start | bytes 1572872 | tf_op jit(solution)/shard_map/ppermute | solution.py:55
  128.2 31.5 %collective-permute-start.12 = (bf16[512,512]{1,0:T(8,128)(2,1)}, bf16[512,512]{1,0:T(8,128)(2,1)}, u32[]{:S(2)}, u32[]{:S(2)}) collective-permute-start(bf16[512,512]{1,0:T(8,128)(2,1)} %slice.219), channel_id=1, source_target_pairs={{0,2},{1,3},{2,4},{3,5},{4,6},{5,7},{6,0},{7,1},{8,10},{9,11},{10,... | collective-permute-start | bytes 1572872 | tf_op jit(solution)/shard_map/ppermute | solution.py:54
  226.6 73.5 %collective-permute-start.14 = (bf16[1024,512]{0,1:T(8,128)(2,1)}, bf16[1024,512]{0,1:T(8,128)(2,1)}, u32[]{:S(2)}, u32[]{:S(2)}) collective-permute-start(bf16[1024,512]{0,1:T(8,128)(2,1)} %bitcast.164), channel_id=1, source_target_pairs={{0,1},{1,0},{2,3},{3,2},{4,5},{5,4},{6,7},{7,6},{8,9},{9,8},{10,11... | collective-permute-start | bytes 3145736 | tf_op jit(solution)/shard_map/ppermute | solution.py:38
  263.2 31.5 %collective-permute-start.19 = (f32[2,128,512]{2,1,0:T(8,128)S(1)}, f32[2,128,512]{2,1,0:T(8,128)}, u32[]{:S(2)}, u32[]{:S(2)}) collective-permute-start(f32[2,128,512]{2,1,0:T(8,128)S(1)} %fusion.56), channel_id=1, source_target_pairs={{0,64},{8,72},{16,80},{24,88},{32,96},{40,104},{48,112},{56,120},{... | collective-permute-start | bytes 1572872 | tf_op jit(solution)/shard_map/ppermute | solution.py:15
  297.1 13.1 %collective-permute-start.20 = (f32[2,128,512]{2,1,0:T(8,128)S(1)}, f32[2,128,512]{2,1,0:T(8,128)S(1)}, u32[]{:S(2)}, u32[]{:S(2)}) collective-permute-start(f32[2,128,512]{2,1,0:T(8,128)S(1)} %fusion.58), channel_id=1, source_target_pairs={{0,32},{8,40},{16,48},{24,56},{32,0},{40,8},{48,16},{56,24},{64,96... | collective-permute-start | bytes 1572872 | tf_op jit(solution)/shard_map/ppermute | solution.py:15
  302.4 53.1 %collective-permute-start.16 = (bf16[1024,1024]{0,1:T(8,128)(2,1)}, bf16[1024,1024]{0,1:T(8,128)(2,1)}, u32[]{:S(2)}, u32[]{:S(2)}) collective-permute-start(bf16[1024,1024]{0,1:T(8,128)(2,1)} %constant_dynamic-update-slice_fusion), channel_id=1, source_target_pairs={{0,2},{1,3},{2,4},{3,5},{4,6},{5,7},{6,0},{7,1},{8,10},{9,11},{10,... | collective-permute-start | bytes 6291464 | tf_op jit(solution)/shard_map/ppermute | solution.py:48
  303.9 55.6 %collective-permute-start.15 = (bf16[1024,1024]{0,1:T(8,128)(2,1)}, bf16[1024,1024]{0,1:T(8,128)(2,1)}, u32[]{:S(2)}, u32[]{:S(2)}) collective-permute-start(bf16[1024,1024]{0,1:T(8,128)(2,1)} %constant_dynamic-update-slice_fusion), channel_id=1, source_target_pairs={{0,6},{1,7},{2,0},{3,1},{4,2},{5,3},{6,4},{7,5},{8,14},{9,15},{10,... | collective-permute-start | bytes 6291464 | tf_op jit(solution)/shard_map/ppermute | solution.py:49
  312.6 40.5 %collective-permute-start.21 = (f32[2,128,512]{2,1,0:T(8,128)}, f32[2,128,512]{2,1,0:T(8,128)}, u32[]{:S(2)}, u32[]{:S(2)}) collective-permute-start(f32[2,128,512]{2,1,0:T(8,128)} %fusion.55), channel_id=1, source_target_pairs={{0,16},{8,24},{16,0},{24,8},{32,48},{40,56},{48,32},{56,40},{64,80... | collective-permute-start | bytes 1572872 | tf_op jit(solution)/shard_map/ppermute | solution.py:15
  358.0 24.7 %collective-permute-start.17 = (bf16[1024,512]{0,1:T(8,128)(2,1)}, bf16[1024,512]{0,1:T(8,128)(2,1)}, u32[]{:S(2)}, u32[]{:S(2)}) collective-permute-start(bf16[1024,512]{0,1:T(8,128)(2,1)} %slice.221), channel_id=1, source_target_pairs={{0,2},{1,3},{2,4},{3,5},{4,6},{5,7},{6,0},{7,1},{8,10},{9,11},{10,... | collective-permute-start | bytes 3145736 | tf_op jit(solution)/shard_map/ppermute | solution.py:54
  361.7 23.3 %collective-permute-start.18 = (bf16[1024,512]{0,1:T(8,128)(2,1)}, bf16[1024,512]{0,1:T(8,128)(2,1)}, u32[]{:S(2)}, u32[]{:S(2)}) collective-permute-start(bf16[1024,512]{0,1:T(8,128)(2,1)} %slice.222), channel_id=1, source_target_pairs={{0,6},{1,7},{2,0},{3,1},{4,2},{5,3},{6,4},{7,5},{8,14},{9,15},{10,... | collective-permute-start | bytes 3145736 | tf_op jit(solution)/shard_map/ppermute | solution.py:55
  364.5 15.3 %collective-permute-start.22 = (f32[2,128,512]{2,1,0:T(8,128)}, f32[2,128,512]{2,1,0:T(8,128)S(1)}, u32[]{:S(2)}, u32[]{:S(2)}) collective-permute-start(f32[2,128,512]{2,1,0:T(8,128)} %fusion.59), channel_id=1, source_target_pairs={{0,8},{8,0},{16,24},{24,16},{32,40},{40,32},{48,56},{56,48},{64,72... | collective-permute-start | bytes 1572872 | tf_op jit(solution)/shard_map/ppermute | solution.py:15
  (48 other events, 417.3 us)
Sparse Core Ops, SparseCore 0:
  102.3 88.2 all-gather.1
  225.2 113.2 reduce-scatter.1
where the time goes:
time: 414 us; the launch traced here: 409 us
  local copies, waits for them, and re-layouts  120 us (29%)
  other arithmetic  115 us (28%)
  matrix products  76 us (18%)
  starting transfers between devices  55.5 us (13%)
  waiting for transfers between devices  26.6 us (6%)
  between operations  15.3 us (4%)
    sub x1, other arithmetic, body(): grad_score = (attn_prob * (grad_prob - row_delta)).astype(jnp.bfloat16)  29.6 us
    unnamed x103, local copies, waits for them, and re-layouts  28.6 us
    ppermute x1, starting transfers between devices, weight_columns(): lax.ppermute(mine, 'seq', [(src, src ^ 1) for src in range(seq_count)])  17.4 us
    ppermute x8, starting transfers between devices, swapped(): return lax.ppermute(value, axis, pairs)  15.9 us
    ppermute x8, waiting for transfers between devices, swapped(): return lax.ppermute(value, axis, pairs)  12.5 us
    slice x2, local copies, waits for them, and re-layouts, body(): value_heads = key_set[1].reshape(blocks, near_keys, head_count, DH)  10 us
    reshape x2, local copies, waits for them, and re-layouts, spread_rows(): return wide.reshape(shape_in[:-2] + (shape_in[-2] * factor, shape_in[-1]))  9.9 us
    ppermute x4, starting transfers between devices, weight_columns(): fetched.append(lax.ppermute(outgoing, ('seq', 'head'), pairs))  9.28 us
  transfers between devices with their start and end apart: 25, of which 6 were waited for; matrix products, arithmetic and copies ran while one was open for 65% of the time, Pallas kernels for 0%

commit v1 on v0

--- a/solution.py
+++ b/solution.py
@@ -218,7 +218,12 @@
     half_rows = row_count // 2
     grads_full = jnp.concatenate(
         [
-            lax.all_gather(cotangent[:half_rows], "head", axis=1, tiled=True),
+            jnp.concatenate(
+                lax.all_to_all(
+                    jnp.stack([cotangent[:half_rows]] * lax.axis_size("head")), "head", 0, 0
+                ),
+                axis=1,
+            ),
             head_ring_gather(cotangent[half_rows:]),
         ],
         axis=0,

time: 414 us -> 435 us (1.051)
  waiting for transfers between devices: 26.6 us -> 42.5 us
    ppermute x2, waiting for transfers between devices: 2.3 us -> 23.9 us  [head_ring_gather(): lax.ppermute(from_above[..., width:], 'head', downward)]
    all_gather x1 -> x0, waiting for transfers between devices: 8.63 us -> none  [body(): lax.all_gather(cotangent[:half_rows], 'head', axis=1, tiled=True)]
    unnamed x103 -> x102, local copies, waits for them, and re-layouts: 28.6 us -> 22.5 us
    all_to_all x0 -> x1, starting transfers between devices: none -> 4.55 us  [body(): lax.all_to_all(jnp.stack([cotangent[:half_rows]] * lax.axis_size('head'))...]
    ppermute x1, starting transfers between devices: 17.4 us -> 12.9 us  [weight_columns(): lax.ppermute(mine, 'seq', [(src, src ^ 1) for src in range(seq_count)])]
  transfers between devices with their start and end apart: 25 -> 25, of which waited for: 6 -> 7; matrix products, arithmetic and copies ran while one was open for 65% -> 63% of each run, Pallas kernels for 0% -> 0%
where the time goes in v1:
time: 435 us; the launch traced here: 429 us
  local copies, waits for them, and re-layouts  121 us (28%)
  other arithmetic  116 us (27%)
  matrix products  78 us (18%)
  starting transfers between devices  56.9 us (13%)
  waiting for transfers between devices  42.5 us (10%)
  between operations  15.5 us (4%)
    sub x1, other arithmetic, body(): grad_score = (attn_prob * (grad_prob - row_delta)).astype(jnp.bfloat16)  29.3 us
    ppermute x2, waiting for transfers between devices, head_ring_gather(): lax.ppermute(from_above[..., width:], 'head', downward)  23.9 us
    unnamed x102, local copies, waits for them, and re-layouts  22.5 us
    ppermute x8, starting transfers between devices, swapped(): return lax.ppermute(value, axis, pairs)  15.2 us
    ppermute x8, waiting for transfers between devices, swapped(): return lax.ppermute(value, axis, pairs)  14.2 us
    ppermute x1, starting transfers between devices, weight_columns(): lax.ppermute(mine, 'seq', [(src, src ^ 1) for src in range(seq_count)])  12.9 us
    dot_general x1, matrix products, body(): lax.dot_general(grads_full, out_weight, (((1,), (1,)), ((), ())), preferr...  10.3 us
    reshape x2, local copies, waits for them, and re-layouts, spread_rows(): return wide.reshape(shape_in[:-2] + (shape_in[-2] * factor, shape_in[-1]))  10.2 us
  transfers between devices with their start and end apart: 25, of which 7 were waited for; matrix products, arithmetic and copies ran while one was open for 63% of the time, Pallas kernels for 0%

profile of v1, /device:TPU:0, one launch (start us, length us, event | category | flops | bytes accessed | tf_op | source)
XLA Modules:
  0.0 429.3 jit_solution(14866917458677267746)
XLA Ops:
  30.9 5.8 %convert_reduce_fusion.2 = f32[2,512,512]{2,1,0:T(8,128)S(1)} fusion(bf16[1,512,2,512]{3,2,1,0:T(2,128)(2,1)S(1)} %copy-done.30, bf16[1,512,2,512]{3,2,1,0:T(2,128)(2,1)S(1)} %copy-done.29), kind=kLoop, calls=%fused_computation.42 | loop fusion | flops 2621440 | bytes 4194304 | tf_op jit(solution)/shard_map/reduce_sum | solution.py:155
  45.0 6.6 %copy.194 = bf16[1,8,512,512]{2,3,1,0:T(8,128)(2,1)} copy(bf16[1,8,512,512]{3,2,1,0:T(8,128)(2,1)} %get-tuple-element.54) | data formatting | bytes 8388608 | tf_op jit(solution)/shard_map/slice | solution.py:188
  58.0 4.6 %convolution_bitcast_fusion.2 = f32[8,4,128,512]{2,3,1,0:T(8,128)} fusion(bf16[8,512,4,128]{1,3,2,0:T(8,128)(2,1)S(1)} %bitcast.168, bf16[8,128,4,128]{1,3,2,0:T(8,128)(2,1)S(1)} %copy.218), kind=kOutput, calls=%fused_computation.57 | convolution fusion | flops 536870912 | bytes 13631488 | tf_op jit(solution)/shard_map/bqhd,bkhd->bhqk/dot_general | solution.py:195
  62.6 8.1 %collective-permute-done.1 = f32[2,128,512]{2,1,0:T(8,128)S(1)} collective-permute-done((f32[2,128,512]{2,1,0:T(8,128)S(1)}, f32[2,128,512]{2,1,0:T(8,128)S(1)}, u32[]{:S(2)}, u32[]{:S(2)}) %collective-permute-start.1) | collective-permute-done | bytes 524320 | tf_op jit(solution)/shard_map/ppermute | solution.py:15
  80.5 6.5 %copy.192 = bf16[1,8,512,512]{2,3,1,0:T(8,128)(2,1)} copy(bf16[1,8,512,512]{3,2,1,0:T(8,128)(2,1)} %get-tuple-element.53) | data formatting | bytes 8388608 | tf_op jit(solution)/shard_map/slice | solution.py:189
  89.4 5.5 %collective-permute-start.7 = (bf16[512,512]{1,0:T(8,128)(2,1)}, bf16[512,512]{1,0:T(8,128)(2,1)}, u32[]{:S(2)}, u32[]{:S(2)}) collective-permute-start(bf16[512,512]{1,0:T(8,128)(2,1)} %get-tuple-element.63), channel_id=1, source_target_pairs={{0,7},{1,0},{2,1},{3,2},{4,3},{5,4},{6,5},{7,6},{16,23},{17,16},{1... | collective-permute-start | bytes 1572872 | tf_op jit(solution)/shard_map/ppermute | solution.py:90
  105.7 12.9 %collective-permute-start.8 = (bf16[4,512,512]{2,1,0:T(8,128)(2,1)}, bf16[4,512,512]{2,1,0:T(8,128)(2,1)}, u32[]{:S(2)}, u32[]{:S(2)}) collective-permute-start(bf16[4,512,512]{2,1,0:T(8,128)(2,1)} %pad_maximum_fusion.10), channel_id=1, source_target_pairs={{0,8},{8,0},{16,24},{24,16},{32,40},{40,32},{48,56},{56,48},{64,72... | collective-permute-start | bytes 6291464 | tf_op jit(solution)/shard_map/ppermute | solution.py:92
  121.0 4.6 %all-to-all-start = ((bf16[8,512,512]{1,2,0:T(8,128)(2,1)}), bf16[8,512,512]{1,2,0:T(8,128)(2,1)}, u32[]{:S(2)}, u32[]{:S(2)}) async-start(bf16[8,512,512]{1,2,0:T(8,128)(2,1)} %stack.112), calls=%async_computation | async-start | bytes 8388608 | tf_op jit(solution)/shard_map/all_to_all | solution.py:222
  138.7 7.8 %fusion.81 = (f32[8,4,128]{2,1,0:T(4,128)S(1)}, f32[8,4,128,1024]{2,3,1,0:T(8,128)S(1)}) fusion(f32[8,4,128,512]{2,3,1,0:T(8,128)S(1)} %convolution_bitcast_fusion.1, f32[8,4,128,512]{2,3,1,0:T(8,128)} %convolution_bitcast_fusion.2, f32[1024]{0:T(1024)S(1)} %copy-done.46, pred[8,1024]{1,0:T(8,128)(4,1)S(1)} %concatenate.89), kind=kOutput, calls=%fused_computation.168 | output fusion | flops 25166848 | bytes 33583104 | tf_op jit(solution)/shard_map/sub | solution.py:209
  162.9 21.6 %collective-permute-done.13 = bf16[512,512]{1,0:T(8,128)(2,1)} collective-permute-done((bf16[512,512]{1,0:T(8,128)(2,1)}, bf16[512,512]{1,0:T(8,128)(2,1)}, u32[]{:S(2)}, u32[]{:S(2)}) %collective-permute-start.13) | collective-permute-done | bytes 524320 | tf_op jit(solution)/shard_map/ppermute | solution.py:55
  189.4 5.0 %gather_fusion = bf16[4,512,1024]{2,1,0:T(8,128)(2,1)} fusion(bf16[4,512,1024]{2,1,0:T(8,128)(2,1)} %pad_maximum_fusion.7, s32[1024]{0:T(1024)S(1)} %pad_clamp_fusion), kind=kCustom, calls=%fused_computation | custom fusion | bytes 8388624 | tf_op jit(solution)/shard_map/gather | solution.py:64
  194.4 6.2 %copy.211 = bf16[512,4,1024]{0,2,1:T(8,128)(2,1)} copy(bf16[512,4,1024]{2,0,1:T(8,128)(2,1)} %bitcast.182) | data formatting | bytes 8388608 | tf_op jit(solution)/shard_map/transpose | solution.py:65
  207.8 10.3 %fusion.45 = bf16[1024,512]{1,0:T(8,128)(2,1)} fusion(bf16[512,4096]{1,0:T(8,128)(2,1)} %param.9, bf16[512,4096]{0,1:T(8,128)(2,1)} %bitcast.197, bf16[512,4096]{0,1:T(8,128)(2,1)} %bitcast.39), kind=kOutput, calls=%fused_computation.82 | convolution fusion | flops 4312268800 | bytes 13631488 | tf_op jit(solution)/shard_map/dot_general | solution.py:231
  218.1 10.1 %fusion.13 = f32[4096,512]{1,0:T(8,128)} fusion(bf16[1024,512]{0,1:T(8,128)(2,1)S(1)} %bitcast.199, bf16[512,4096]{0,1:T(8,128)(2,1)S(1)} %bitcast.198, bf16[512,4096]{0,1:T(8,128)(2,1)} %bitcast.39), kind=kOutput, calls=%fused_computation.25 | convolution fusion | flops 4311744512 | bytes 17825792 | tf_op jit(solution)/shard_map/dot_general | solution.py:237
  230.4 5.1 %fusion.20 = f32[4,128,512,1]{2,1,3,0:T(8,128)} fusion(bf16[8,128,4,128]{3,2,1,0:T(4,128)(2,1)S(1)} %reshape.250, bf16[8,4,128,1024]{2,3,1,0:T(8,128)(2,1)} %fusion.70), kind=kOutput, calls=%fused_computation.37 | convolution fusion | flops 536870912 | bytes 6291456 | tf_op jit(solution)/shard_map/bhqk,bqhd->khd/dot_general | solution.py:286
  235.5 4.6 %fusion.82 = f32[8,4,128,512]{2,3,1,0:T(8,128)} fusion(bf16[8,128,4,128]{1,3,2,0:T(8,128)(2,1)S(1)} %copy.237, bf16[8,512,4,128]{1,3,2,0:T(8,128)(2,1)S(1)} %bitcast.179), kind=kOutput, calls=%fused_computation.169 | convolution fusion | flops 536870912 | bytes 13631488 | tf_op jit(solution)/shard_map/bqhd,bkhd->bhqk/dot_general | solution.py:247
  240.1 4.6 %convolution_bitcast_fusion = f32[8,4,128,512]{2,3,1,0:T(8,128)} fusion(bf16[512,4,128,1]{0,2,1,3:T(8,128)(2,1)S(1)} %bitcast.191, bf16[8,128,4,128]{1,3,2,0:T(8,128)(2,1)S(1)} %copy.237), kind=kOutput, calls=%fused_computation.55 | convolution fusion | flops 536870912 | bytes 9961472 | tf_op jit(solution)/shard_map/bqhd,khd->bhqk/dot_general | solution.py:250
  247.9 29.3 %multiply_convert_fusion = bf16[8,4,128,1024]{2,3,1,0:T(8,128)(2,1)} fusion(f32[8,4,128,512]{2,3,1,0:T(8,128)} %convolution_bitcast_fusion, f32[8,4,128,512]{2,3,1,0:T(8,128)} %fusion.82, f32[8,4,128,1024]{2,3,1,0:T(8,128)} %copy-done.12, f32[8,4,128]{2,1,0:T(4,128)S(1)} %get-tuple-element.94), kind=kOutput, calls=%fused_computation.13 | output fusion | flops 33559552 | bytes 41959424 | tf_op jit(solution)/shard_map/sub | solution.py:257
  277.2 4.6 %fusion.49 = f32[4,512,128]{1,2,0:T(8,128)} fusion(bf16[8,128,4,128]{1,3,2,0:T(8,128)(2,1)S(1)} %copy-done.9, bf16[8,4,128,1024]{2,3,1,0:T(8,128)(2,1)} %multiply_convert_fusion), kind=kOutput, calls=%fused_computation.84 | convolution fusion | flops 537133056 | bytes 6291456 | tf_op jit(solution)/shard_map/bhqk,bqhd->khd/dot_general | solution.py:283
  294.4 7.2 %fusion.16 = (f32[2,8,128,512]{2,3,1,0:T(8,128)}, f32[2,8,128,512]{2,3,1,0:T(8,128)}, f32[2,8,128,512]{2,3,1,0:T(8,128)}, f32[2,8,128,512]{2,3,1,0:T(8,128)}) fusion(f32[1,8,512,512]{2,3,1,0:T(8,128)S(1)} %bitcast.181, f32[1,8,512,512]{2,3,1,0:T(8,128)S(1)} %bitcast.180), kind=kLoop, calls=%fused_computation.28 | loop fusion | flops 4194304 | bytes 33554432 | tf_op jit(solution)/shard_map/stack | solution.py:281
  305.3 4.2 fusion.39
  324.8 6.1 %collective-permute-done.20 = f32[2,128,512]{2,1,0:T(8,128)S(1)} collective-permute-done((f32[2,128,512]{2,1,0:T(8,128)S(1)}, f32[2,128,512]{2,1,0:T(8,128)S(1)}, u32[]{:S(2)}, u32[]{:S(2)}) %collective-permute-start.20) | collective-permute-done | bytes 524320 | tf_op jit(solution)/shard_map/ppermute | solution.py:15
  342.2 5.4 %copy.239 = f32[2,8,128,512]{3,2,1,0:T(8,128)} copy(f32[2,8,128,512]{2,3,1,0:T(8,128)} %get-tuple-element.49) | data formatting | bytes 8388608 | tf_op jit(solution)/shard_map/slice | solution.py:290
  389.3 6.5 %reshape.264 = f32[2,1024,512]{2,1,0:T(8,128)} reshape(f32[2,512,2,512]{3,2,1,0:T(2,128)} %broadcast_in_dim.45) | data formatting | bytes 8388608 | tf_op jit(solution)/shard_map/reshape | solution.py:29
  (260 shorter events, 220.5 us)
Async XLA Ops:
  9.0 65.8 %collective-permute-start.9 = (bf16[512,512]{1,0:T(8,128)(2,1)}, bf16[512,512]{1,0:T(8,128)(2,1)}, u32[]{:S(2)}, u32[]{:S(2)}) collective-permute-start(bf16[512,512]{1,0:T(8,128)(2,1)} %slice.169), channel_id=1, source_target_pairs={{0,1},{1,0},{2,3},{3,2},{4,5},{5,4},{6,7},{7,6},{8,9},{9,8},{10,11... | collective-permute-start | bytes 1572872 | tf_op jit(solution)/shard_map/ppermute | solution.py:38
  14.5 37.1 %collective-permute-start = (f32[2,128,512]{2,1,0:T(8,128)}, f32[2,128,512]{2,1,0:T(8,128)}, u32[]{:S(2)}, u32[]{:S(2)}) collective-permute-start(f32[2,128,512]{2,1,0:T(8,128)} %broadcast_multiply_fusion.3), channel_id=1, source_target_pairs={{0,8},{8,0},{16,24},{24,16},{32,40},{40,32},{48,56},{56,48},{64,72... | collective-permute-start | bytes 1572872 | tf_op jit(solution)/shard_map/ppermute | solution.py:15
  17.8 71.6 %collective-permute-start.6 = (bf16[512,512]{1,0:T(8,128)(2,1)}, bf16[512,512]{1,0:T(8,128)(2,1)}, u32[]{:S(2)}, u32[]{:S(2)}) collective-permute-start(bf16[512,512]{1,0:T(8,128)(2,1)} %get-tuple-element.60), channel_id=1, source_target_pairs={{0,5},{1,6},{2,7},{3,0},{4,1},{5,2},{6,3},{7,4},{8,14},{9,15},{10,... | collective-permute-start | bytes 1572872 | tf_op jit(solution)/shard_map/ppermute | solution.py:90
  21.0 75.3 %collective-permute-start.5 = (bf16[512,512]{1,0:T(8,128)(2,1)}, bf16[512,512]{1,0:T(8,128)(2,1)}, u32[]{:S(2)}, u32[]{:S(2)}) collective-permute-start(bf16[512,512]{1,0:T(8,128)(2,1)} %get-tuple-element.61), channel_id=1, source_target_pairs={{0,3},{1,4},{2,5},{3,6},{4,7},{5,0},{6,1},{7,2},{8,12},{9,13},{10,... | collective-permute-start | bytes 1572872 | tf_op jit(solution)/shard_map/ppermute | solution.py:90
  54.9 15.8 %collective-permute-start.1 = (f32[2,128,512]{2,1,0:T(8,128)S(1)}, f32[2,128,512]{2,1,0:T(8,128)S(1)}, u32[]{:S(2)}, u32[]{:S(2)}) collective-permute-start(f32[2,128,512]{2,1,0:T(8,128)S(1)} %copy_multiply_fusion.2), channel_id=1, source_target_pairs={{0,16},{8,24},{16,0},{24,8},{32,48},{40,56},{48,32},{56,40},{64,80... | collective-permute-start | bytes 1572872 | tf_op jit(solution)/shard_map/ppermute | solution.py:15
  72.9 14.0 %collective-permute-start.2 = (f32[2,128,512]{2,1,0:T(8,128)}, f32[2,128,512]{2,1,0:T(8,128)}, u32[]{:S(2)}, u32[]{:S(2)}) collective-permute-start(f32[2,128,512]{2,1,0:T(8,128)} %copy_multiply_fusion.1), channel_id=1, source_target_pairs={{0,32},{8,40},{16,48},{24,56},{32,0},{40,8},{48,16},{56,24},{64,96... | collective-permute-start | bytes 1572872 | tf_op jit(solution)/shard_map/ppermute | solution.py:15
  78.4 49.4 %collective-permute-start.10 = (bf16[512,1024]{1,0:T(8,128)(2,1)}, bf16[512,1024]{1,0:T(8,128)(2,1)S(1)}, u32[]{:S(2)}, u32[]{:S(2)}) collective-permute-start(bf16[512,1024]{1,0:T(8,128)(2,1)} %get-tuple-element.87), channel_id=1, source_target_pairs={{0,6},{1,7},{2,0},{3,1},{4,2},{5,3},{6,4},{7,5},{8,14},{9,15},{10,... | collective-permute-start | bytes 3145736 | tf_op jit(solution)/shard_map/ppermute | solution.py:49
  79.5 52.3 %collective-permute-start.11 = (bf16[512,1024]{1,0:T(8,128)(2,1)}, bf16[512,1024]{1,0:T(8,128)(2,1)S(1)}, u32[]{:S(2)}, u32[]{:S(2)}) collective-permute-start(bf16[512,1024]{1,0:T(8,128)(2,1)} %get-tuple-element.87), channel_id=1, source_target_pairs={{0,2},{1,3},{2,4},{3,5},{4,6},{5,7},{6,0},{7,1},{8,10},{9,11},{10,... | collective-permute-start | bytes 3145736 | tf_op jit(solution)/shard_map/ppermute | solution.py:48
  87.0 15.0 %collective-permute-start.4 = (bf16[512,512]{1,0:T(8,128)(2,1)}, bf16[512,512]{1,0:T(8,128)(2,1)}, u32[]{:S(2)}, u32[]{:S(2)}) collective-permute-start(bf16[512,512]{1,0:T(8,128)(2,1)} %get-tuple-element.62), channel_id=1, source_target_pairs={{0,1},{1,2},{2,3},{3,4},{4,5},{5,6},{6,7},{7,0},{8,10},{9,11},{10,... | collective-permute-start | bytes 1572872 | tf_op jit(solution)/shard_map/ppermute | solution.py:90
  89.4 13.2 %collective-permute-start.7 = (bf16[512,512]{1,0:T(8,128)(2,1)}, bf16[512,512]{1,0:T(8,128)(2,1)}, u32[]{:S(2)}, u32[]{:S(2)}) collective-permute-start(bf16[512,512]{1,0:T(8,128)(2,1)} %get-tuple-element.63), channel_id=1, source_target_pairs={{0,7},{1,0},{2,1},{3,2},{4,3},{5,4},{6,5},{7,6},{16,23},{17,16},{1... | collective-permute-start | bytes 1572872 | tf_op jit(solution)/shard_map/ppermute | solution.py:90
  96.2 37.7 %collective-permute-start.3 = (bf16[2,128,512]{2,1,0:T(8,128)(2,1)S(1)}, bf16[2,128,512]{2,1,0:T(8,128)(2,1)}, u32[]{:S(2)}, u32[]{:S(2)}) collective-permute-start(bf16[2,128,512]{2,1,0:T(8,128)(2,1)S(1)} %copy_multiply_fusion), channel_id=1, source_target_pairs={{0,64},{8,72},{16,80},{24,88},{32,96},{40,104},{48,112},{56,120},{... | collective-permute-start | bytes 786440 | tf_op jit(solution)/shard_map/ppermute | solution.py:15
  105.7 94.9 %collective-permute-start.8 = (bf16[4,512,512]{2,1,0:T(8,128)(2,1)}, bf16[4,512,512]{2,1,0:T(8,128)(2,1)}, u32[]{:S(2)}, u32[]{:S(2)}) collective-permute-start(bf16[4,512,512]{2,1,0:T(8,128)(2,1)} %pad_maximum_fusion.10), channel_id=1, source_target_pairs={{0,8},{8,0},{16,24},{24,16},{32,40},{40,32},{48,56},{56,48},{64,72... | collective-permute-start | bytes 6291464 | tf_op jit(solution)/shard_map/ppermute | solution.py:92
  121.0 86.8 %all-to-all-start = ((bf16[8,512,512]{1,2,0:T(8,128)(2,1)}), bf16[8,512,512]{1,2,0:T(8,128)(2,1)}, u32[]{:S(2)}, u32[]{:S(2)}) async-start(bf16[8,512,512]{1,2,0:T(8,128)(2,1)} %stack.112), calls=%async_computation | async-start | bytes 8388608 | tf_op jit(solution)/shard_map/all_to_all | solution.py:222
  125.6 296.4 %reduce-scatter.2.cloned.1.call-start = ((), (), s32[]{:S(2)}) async-start(), calls=%async_computation.2 | async-start | bytes 8912896 | tf_op jit(solution)/shard_map/reduce_scatter | solution.py:236
  128.7 55.9 %collective-permute-start.13 = (bf16[512,512]{1,0:T(8,128)(2,1)}, bf16[512,512]{1,0:T(8,128)(2,1)}, u32[]{:S(2)}, u32[]{:S(2)}) collective-permute-start(bf16[512,512]{1,0:T(8,128)(2,1)} %slice.220), channel_id=1, source_target_pairs={{0,6},{1,7},{2,0},{3,1},{4,2},{5,3},{6,4},{7,5},{8,14},{9,15},{10,... | collective-permute-start | bytes 1572872 | tf_op jit(solution)/shard_map/ppermute | solution.py:55
  132.7 53.1 %collective-permute-start.12 = (bf16[512,512]{1,0:T(8,128)(2,1)}, bf16[512,512]{1,0:T(8,128)(2,1)}, u32[]{:S(2)}, u32[]{:S(2)}) collective-permute-start(bf16[512,512]{1,0:T(8,128)(2,1)} %slice.219), channel_id=1, source_target_pairs={{0,2},{1,3},{2,4},{3,5},{4,6},{5,7},{6,0},{7,1},{8,10},{9,11},{10,... | collective-permute-start | bytes 1572872 | tf_op jit(solution)/shard_map/ppermute | solution.py:54
  246.3 72.9 %collective-permute-start.14 = (bf16[1024,512]{0,1:T(8,128)(2,1)}, bf16[1024,512]{0,1:T(8,128)(2,1)}, u32[]{:S(2)}, u32[]{:S(2)}) collective-permute-start(bf16[1024,512]{0,1:T(8,128)(2,1)} %bitcast.200), channel_id=1, source_target_pairs={{0,1},{1,0},{2,3},{3,2},{4,5},{5,4},{6,7},{7,6},{8,9},{9,8},{10,11... | collective-permute-start | bytes 3145736 | tf_op jit(solution)/shard_map/ppermute | solution.py:38
  283.5 32.1 %collective-permute-start.19 = (f32[2,128,512]{2,1,0:T(8,128)S(1)}, f32[2,128,512]{2,1,0:T(8,128)}, u32[]{:S(2)}, u32[]{:S(2)}) collective-permute-start(f32[2,128,512]{2,1,0:T(8,128)S(1)} %fusion.56), channel_id=1, source_target_pairs={{0,64},{8,72},{16,80},{24,88},{32,96},{40,104},{48,112},{56,120},{... | collective-permute-start | bytes 1572872 | tf_op jit(solution)/shard_map/ppermute | solution.py:15
  321.5 54.7 %collective-permute-start.16 = (bf16[1024,1024]{0,1:T(8,128)(2,1)}, bf16[1024,1024]{0,1:T(8,128)(2,1)}, u32[]{:S(2)}, u32[]{:S(2)}) collective-permute-start(bf16[1024,1024]{0,1:T(8,128)(2,1)} %constant_dynamic-update-slice_fusion), channel_id=1, source_target_pairs={{0,2},{1,3},{2,4},{3,5},{4,6},{5,7},{6,0},{7,1},{8,10},{9,11},{10,... | collective-permute-start | bytes 6291464 | tf_op jit(solution)/shard_map/ppermute | solution.py:48
  322.0 57.7 %collective-permute-start.15 = (bf16[1024,1024]{0,1:T(8,128)(2,1)}, bf16[1024,1024]{0,1:T(8,128)(2,1)}, u32[]{:S(2)}, u32[]{:S(2)}) collective-permute-start(bf16[1024,1024]{0,1:T(8,128)(2,1)} %constant_dynamic-update-slice_fusion), channel_id=1, source_target_pairs={{0,6},{1,7},{2,0},{3,1},{4,2},{5,3},{6,4},{7,5},{8,14},{9,15},{10,... | collective-permute-start | bytes 6291464 | tf_op jit(solution)/shard_map/ppermute | solution.py:49
  333.3 40.5 %collective-permute-start.21 = (f32[2,128,512]{2,1,0:T(8,128)}, f32[2,128,512]{2,1,0:T(8,128)}, u32[]{:S(2)}, u32[]{:S(2)}) collective-permute-start(f32[2,128,512]{2,1,0:T(8,128)} %fusion.55), channel_id=1, source_target_pairs={{0,16},{8,24},{16,0},{24,8},{32,48},{40,56},{48,32},{56,40},{64,80... | collective-permute-start | bytes 1572872 | tf_op jit(solution)/shard_map/ppermute | solution.py:15
  378.7 24.5 %collective-permute-start.17 = (bf16[1024,512]{0,1:T(8,128)(2,1)}, bf16[1024,512]{0,1:T(8,128)(2,1)}, u32[]{:S(2)}, u32[]{:S(2)}) collective-permute-start(bf16[1024,512]{0,1:T(8,128)(2,1)} %slice.221), channel_id=1, source_target_pairs={{0,2},{1,3},{2,4},{3,5},{4,6},{5,7},{6,0},{7,1},{8,10},{9,11},{10,... | collective-permute-start | bytes 3145736 | tf_op jit(solution)/shard_map/ppermute | solution.py:54
  382.0 23.6 %collective-permute-start.18 = (bf16[1024,512]{0,1:T(8,128)(2,1)}, bf16[1024,512]{0,1:T(8,128)(2,1)}, u32[]{:S(2)}, u32[]{:S(2)}) collective-permute-start(bf16[1024,512]{0,1:T(8,128)(2,1)} %slice.222), channel_id=1, source_target_pairs={{0,6},{1,7},{2,0},{3,1},{4,2},{5,3},{6,4},{7,5},{8,14},{9,15},{10,... | collective-permute-start | bytes 3145736 | tf_op jit(solution)/shard_map/ppermute | solution.py:55
  385.3 15.3 %collective-permute-start.22 = (f32[2,128,512]{2,1,0:T(8,128)}, f32[2,128,512]{2,1,0:T(8,128)S(1)}, u32[]{:S(2)}, u32[]{:S(2)}) collective-permute-start(f32[2,128,512]{2,1,0:T(8,128)} %fusion.59), channel_id=1, source_target_pairs={{0,8},{8,0},{16,24},{24,16},{32,40},{40,32},{48,56},{56,48},{64,72... | collective-permute-start | bytes 1572872 | tf_op jit(solution)/shard_map/ppermute | solution.py:15
  (48 other events, 534.6 us)
Sparse Core Ops, SparseCore 0:
  244.9 114.4 reduce-scatter.1
